TPU v7x, 512 devices: a whole 4x4x16 slice. The times are simulated.
512 devices in a mesh: sec: 2 (over core), seq: 32 (over z, y_lo), rep: 8 (over x, y_hi).
Axes of the slice: x: 4, y: 4 (y_hi: 2, y_lo: 2; y = y_hi * 2 + y_lo), z: 16, core: 2. Of those that a mesh axis runs over, the one named last changes fastest.
Arguments:
- head_query: bfloat16 [64, 24, 1536, 128], P(('sec', 'rep'), None, 'seq'), may hold values from -4.5 to 4.5
- head_keys: bfloat16 [64, 24, 1536, 128], P(('sec', 'rep'), None, 'seq'), may hold values from -4.5 to 4.5
- head_values: bfloat16 [64, 24, 1536, 128], P(('sec', 'rep'), None, 'seq'), may hold values from -6 to 6
- mod_shift: float32 [64, 3072], P(('sec', 'rep')), may hold values from -3 to 3
- mod_scale: float32 [64, 3072], P(('sec', 'rep')), may hold values from -0.9 to 0.9
- final_weight: bfloat16 [3072, 64], replicated, may hold values from -0.109375 to 0.109375
- final_bias: float32 [64], replicated, may hold values from -3 to 3
- noisy_latent: float32 [64, 3, 64, 512], P(('sec', 'rep'), None, 'seq'), may hold values from -7.2 to 7.2
- step_index: int32 [64], P(('sec', 'rep')), may hold values from 46 to 49
- clip_order: int32 [64], replicated, may hold values from 0 to 63, each once
- conv_weight: bfloat16 [3, 3, 3, 16, 512], replicated, may hold values from -0.3125 to 0.3125
- conv_bias: float32 [512], replicated, may hold values from -3 to 3
- group_gain: float32 [512], replicated, may hold values from 0.1 to 1.9
- group_shift: float32 [512], replicated, may hold values from -3 to 3
Outputs:
- denoised: float32 [64, 3, 64, 512], P(('sec', 'rep'), None, 'seq')
- features: bfloat16 [64, 3, 64, 16384], P(('sec', 'rep'), None, 'seq')
All inputs are finite; a program needn't handle non-finite values.
Results may differ from a plain program's by a relative error of at most 0.005.
Values may be sent and summed in bfloat16 or wider, within the bound.
No kernel may reach another device: no remote copies, remote signals or barrier semaphores. Data moves between devices by JAX's collectives and lax.ppermute only.
A program may use at most 128 MiB of HBM per device.

v0:
```python
import math
import jax
import jax.numpy as jnp
from jax import lax
from jax.sharding import PartitionSpec as P

HEADS = 24
HEAD_DIM = 128
LAT_CH = 16
VAE_CH = 512
GROUPS = 32
FRAMES = 3
PATCH_W = 16
NSTEPS = 50
PATCH_OUT = 64
LAT_W = 32
eps_norm = 1e-06
shift_factor = 7.0


def extended(cells, sides, width):
    for axis, dim in sides:
        count = lax.axis_size(axis)
        ends = count - 1
        head = lax.slice_in_dim(cells, 0, width, axis=dim)
        tail = lax.slice_in_dim(cells, cells.shape[dim] - width, cells.shape[dim], axis=dim)
        cells = jnp.concatenate(
            [
                lax.ppermute(tail, axis, [(i, (i + 1) % count) for i in range(ends)]),
                cells,
                lax.ppermute(head, axis, [((i + 1) % count, i) for i in range(ends)]),
            ],
            axis=dim,
        )
    return cells


def attend_unit(operands):
    query_rows, key_rows, value_rows = operands
    length = query_rows.shape[0]
    block = math.gcd(length, 512)
    scale = 1.0 / math.sqrt(query_rows.shape[1])
    blocks = query_rows.reshape(length // block, block, query_rows.shape[1])

    def one_block(rows):
        scores = jnp.dot(rows, key_rows.T, preferred_element_type=jnp.float32) * scale
        top = jnp.max(scores, axis=1, keepdims=True)
        expd = jnp.exp(scores - top)
        weights = (expd / jnp.sum(expd, axis=1, keepdims=True)).astype(jnp.bfloat16)
        return jnp.dot(weights, value_rows, preferred_element_type=jnp.float32).astype(jnp.bfloat16)

    return lax.map(one_block, blocks).reshape(length, query_rows.shape[1])


def sigma_level(index):
    level = 1.0 - index.astype(jnp.float32) / NSTEPS
    return shift_factor * level / (1.0 + (shift_factor - 1.0) * level)


def causal_columns(rimmed):
    clips, frames, rows_rim, wide = rimmed.shape
    width = wide // LAT_CH
    grid = rimmed.reshape(clips, frames, rows_rim, width, LAT_CH)
    first = grid[:, :1]
    grid = jnp.concatenate([first, first, grid], axis=1)
    grid = jnp.pad(grid, ((0, 0), (0, 0), (0, 0), (1, 1), (0, 0)), mode="edge")
    taps = []
    for tap_time in range(3):
        for tap_row in range(3):
            for tap_col in range(3):
                taps.append(
                    grid[
                        :,
                        tap_time : tap_time + frames,
                        tap_row : tap_row + rows_rim - 2,
                        tap_col : tap_col + width,
                        :,
                    ]
                )
    return jnp.stack(taps, axis=4).reshape(clips, frames, rows_rim - 2, width, 27 * LAT_CH)


def edge_rows(rimmed):
    position = lax.axis_index("seq")
    last_index = lax.axis_size("seq") - 1
    upper = jnp.where(position == 0, rimmed[:, :, 1:2], rimmed[:, :, 0:1])
    lower = jnp.where(position == last_index, rimmed[:, :, -2:-1], rimmed[:, :, -1:])
    return jnp.concatenate([upper, rimmed[:, :, 1:-1], lower], axis=2)


def shards(
    head_query,
    head_keys,
    head_values,
    mod_shift,
    mod_scale,
    final_weight,
    final_bias,
    noisy_latent,
    step_index,
    clip_order,
    conv_weight,
    conv_bias,
    group_gain,
    group_shift,
):
    n_seq = lax.axis_size("seq")
    clips = head_query.shape[0]
    tok_dev = head_query.shape[2]
    units_local = clips * HEADS // n_seq
    query_four = head_query.reshape(n_seq, units_local, tok_dev, HEAD_DIM)
    keys_four = head_keys.reshape(n_seq, units_local, tok_dev, HEAD_DIM)
    values_four = head_values.reshape(n_seq, units_local, tok_dev, HEAD_DIM)
    query_part = lax.all_to_all(query_four, "seq", split_axis=0, concat_axis=2, tiled=True)
    keys_part = lax.all_to_all(keys_four, "seq", split_axis=0, concat_axis=2, tiled=True)
    values_part = lax.all_to_all(values_four, "seq", split_axis=0, concat_axis=2, tiled=True)
    outputs = lax.map(attend_unit, (query_part[0], keys_part[0], values_part[0]))[None]
    mixed = lax.all_to_all(outputs, "seq", split_axis=2, concat_axis=0, tiled=True)
    weights3 = final_weight.astype(jnp.float32).reshape(HEADS, HEAD_DIM, PATCH_OUT)
    scale3 = mod_scale.reshape(clips, HEADS, HEAD_DIM)
    shift3 = mod_shift.reshape(clips, HEADS, HEAD_DIM)
    heads = mixed.reshape(clips, HEADS, tok_dev, HEAD_DIM).astype(jnp.float32)
    mean = jnp.mean(heads, axis=(1, 3), keepdims=True)
    spread = jnp.mean(jnp.square(heads - mean), axis=(1, 3), keepdims=True)
    normed = (heads - mean) * lax.rsqrt(spread + eps_norm)
    modulated = normed * (1.0 + scale3[:, :, None, :]) + shift3[:, :, None, :]
    velocity = (
        jnp.einsum("chtd,hdo->cto", modulated, weights3, precision=lax.Precision.HIGHEST)
        + final_bias
    )
    rows_dev = noisy_latent.shape[2]
    velocity = velocity.reshape(clips, rows_dev // 2, FRAMES, PATCH_W, 2, 2, LAT_CH)
    velocity = jnp.transpose(velocity, (0, 2, 1, 4, 3, 5, 6)).reshape(noisy_latent.shape)
    step = sigma_level(step_index + 1) - sigma_level(step_index)
    denoised = noisy_latent + step[:, None, None, None] * velocity
    decoder_in = denoised.astype(jnp.bfloat16)
    group_index = lax.axis_index(("sec", "rep"))
    wanted = lax.dynamic_slice_in_dim(clip_order, group_index * clips, clips)
    everyone = lax.all_gather(decoder_in, ("sec", "rep"), axis=0, tiled=True)
    picked = jnp.take(everyone, wanted, axis=0)
    rimmed = edge_rows(extended(picked, (("seq", 2),), 1))
    columns = causal_columns(rimmed)
    flat_weight = conv_weight.reshape(27 * LAT_CH, VAE_CH)
    conv_out = (
        jnp.dot(columns.reshape(-1, 27 * LAT_CH), flat_weight, preferred_element_type=jnp.float32)
        + conv_bias
    )
    conv_out = conv_out.reshape(clips, -1, GROUPS, VAE_CH // GROUPS)
    cells = conv_out.shape[1] * n_seq * (VAE_CH // GROUPS)
    local_sum = jnp.sum(conv_out, axis=(1, 3))
    mean = lax.psum(local_sum, "seq") / cells
    centered = conv_out - mean[:, None, :, None]
    spread = lax.psum(jnp.sum(jnp.square(centered), axis=(1, 3)), "seq") / cells
    normed = (centered * lax.rsqrt(spread + eps_norm)[:, None, :, None]).reshape(clips, -1, VAE_CH)
    features = jax.nn.silu(normed * group_gain + group_shift).astype(jnp.bfloat16)
    features = features.reshape(clips, FRAMES, rows_dev, LAT_W * VAE_CH)
    return (denoised, features)


def solution(mesh):
    placed = (
        P(("sec", "rep"), None, "seq", None),
        P(("sec", "rep"), None, "seq", None),
        P(("sec", "rep"), None, "seq", None),
        P(("sec", "rep"), None),
        P(("sec", "rep"), None),
        P(),
        P(),
        P(("sec", "rep"), None, "seq", None),
        P(("sec", "rep")),
        P(),
        P(),
        P(),
        P(),
        P(),
    )
    return jax.shard_map(
        shards,
        mesh=mesh,
        in_specs=placed,
        out_specs=(P(("sec", "rep"), None, "seq", None), P(("sec", "rep"), None, "seq", None)),
        check_vma=False,
    )
```

profile of v0, /device:TPU:8, one launch (start us, length us, event | category | flops | bytes accessed | tf_op | source)
XLA Modules:
  0.0 569.3 jit_solution(6883211467850710125)
XLA Ops:
  0.7 77.9 %all_to_all.54 = bf16[32,3,48,128]{3,2,1,0:T(8,128)(2,1)} all-to-all(bf16[32,3,48,128]{3,2,1,0:T(8,128)(2,1)} %bitcast.227), channel_id=1, replica_groups=mesh['sec'=2,'seq'=32,'rep'=8] {'seq'}, dimensions={0} | all-to-all | bytes 2359296 | tf_op jit(solution)/shard_map/all_to_all | solution.py:114
  78.5 64.2 %all_to_all.55 = bf16[32,3,48,128]{3,2,1,0:T(8,128)(2,1)} all-to-all(bf16[32,3,48,128]{3,2,1,0:T(8,128)(2,1)S(1)} %bitcast.228), channel_id=1, replica_groups=mesh['sec'=2,'seq'=32,'rep'=8] {'seq'}, dimensions={0} | all-to-all | bytes 2359296 | tf_op jit(solution)/shard_map/all_to_all | solution.py:115
  142.7 4.2 all-to-all-start.2
  146.9 1.4 copy.116
  148.5 1.1 copy.117
  149.6 55.0 %all-to-all-done.2 = bf16[32,3,48,128]{3,2,1,0:T(8,128)(2,1)S(1)} async-done(((bf16[32,3,48,128]{3,2,1,0:T(8,128)(2,1)}), bf16[32,3,48,128]{3,2,1,0:T(8,128)(2,1)S(1)}, u32[]{:S(2)}, u32[]{:S(2)}) %all-to-all-start.2) | async-done | bytes 1179680 | tf_op jit(solution)/shard_map/all_to_all | solution.py:116
  204.6 1.1 copy.118
  205.8 24.2 %while.21 = (s32[]{:T(128)}, bf16[3,1536,128]{2,1,0:T(8,128)(2,1)}, bf16[3,1536,128]{2,1,0:T(8,128)(2,1)S(1)}, bf16[3,1536,128]{2,1,0:T(8,128)(2,1)}, bf16[3,153...) while((s32[]{:T(128)}, bf16[3,1536,128]{2,1,0:T(8,128)(2,1)}, ...), condition=%wide.region_5.6_spmd, body=%wide.region_0.5_spmd.sunk | while | flops 408222720 | bytes 13641974 | solution.py:117
  205.8 1.2 dynamic-slice_bitcast_fusion.3
  207.0 6.1 %while.22 = (s32[]{:T(128)}, bf16[3,512,128]{2,1,0:T(8,128)(2,1)S(1)}, bf16[3,512,128]{2,1,0:T(8,128)(2,1)S(1)}, bf16[1536,128]{1,0:T(8,128)(2,1)S(1)}, bf16[1536,128]{1,0:T(8,128)(2,1)S(1)}, /*index=5*/s32[]{:T(128)}) while((s32[]{:T(128)}, bf16[3,512,128]{2,1,0:T(8,128)(2,1)S(1)}, bf16[3,512,128]{2,1,0:T(8,128)(2,1)S(1)}, ...), condition=%wide.region_4.4_spmd, body=%wide.region_1.3_spmd.sunk | while | flops 408222720 | bytes 10496085 | solution.py:52
  208.2 0.8 fusion.89
  210.2 0.8 fusion.89
  212.2 0.8 fusion.89
  213.0 0.8 bitcast_dynamic-update-slice_fusion.2
  213.8 1.2 dynamic-slice_bitcast_fusion.3
  215.0 6.1 %while.22 = (s32[]{:T(128)}, bf16[3,512,128]{2,1,0:T(8,128)(2,1)S(1)}, bf16[3,512,128]{2,1,0:T(8,128)(2,1)S(1)}, bf16[1536,128]{1,0:T(8,128)(2,1)S(1)}, bf16[1536,128]{1,0:T(8,128)(2,1)S(1)}, /*index=5*/s32[]{:T(128)}) while((s32[]{:T(128)}, bf16[3,512,128]{2,1,0:T(8,128)(2,1)S(1)}, bf16[3,512,128]{2,1,0:T(8,128)(2,1)S(1)}, ...), condition=%wide.region_4.4_spmd, body=%wide.region_1.3_spmd.sunk | while | flops 408222720 | bytes 10496085 | solution.py:52
  216.3 0.8 fusion.89
  218.3 0.8 fusion.89
  220.3 0.8 fusion.89
  221.1 0.8 bitcast_dynamic-update-slice_fusion.2
  221.9 1.2 dynamic-slice_bitcast_fusion.3
  223.1 6.1 %while.22 = (s32[]{:T(128)}, bf16[3,512,128]{2,1,0:T(8,128)(2,1)S(1)}, bf16[3,512,128]{2,1,0:T(8,128)(2,1)S(1)}, bf16[1536,128]{1,0:T(8,128)(2,1)S(1)}, bf16[1536,128]{1,0:T(8,128)(2,1)S(1)}, /*index=5*/s32[]{:T(128)}) while((s32[]{:T(128)}, bf16[3,512,128]{2,1,0:T(8,128)(2,1)S(1)}, bf16[3,512,128]{2,1,0:T(8,128)(2,1)S(1)}, ...), condition=%wide.region_4.4_spmd, body=%wide.region_1.3_spmd.sunk | while | flops 408222720 | bytes 10496085 | solution.py:52
  224.3 0.8 fusion.89
  226.3 0.8 fusion.89
  228.4 0.8 fusion.89
  229.1 0.8 bitcast_dynamic-update-slice_fusion.2
  229.9 8.1 %copy.141 = bf16[3,1536,128]{2,0,1:T(4,128)(2,1)} copy(bf16[3,1536,128]{2,1,0:T(8,128)(2,1)} %get-tuple-element.56) | data formatting | bytes 2359296 | tf_op jit(solution)/shard_map/while | solution.py:117
  238.1 5.7 all-to-all-start.3
  243.9 76.1 %all-to-all-done.3 = bf16[1,3,1536,128]{3,1,0,2:T(4,128)(2,1)S(1)} async-done(((bf16[1,3,1536,128]{3,1,0,2:T(4,128)(2,1)}), bf16[1,3,1536,128]{3,1,0,2:T(4,128)(2,1)S(1)}, u32[]{:S(2)}, u32[]{:S(2)}) %all-to-all-start.3) | async-done | bytes 1179680 | tf_op jit(solution)/shard_map/all_to_all | solution.py:118
  320.4 3.1 fusion.19
  323.7 22.0 %multiply_reduce_fusion = f32[32,48]{1,0:T(8,128)S(1)} fusion(bf16[1,3,32,48,128]{4,1,3,2,0:T(4,128)(2,1)S(1)} %bitcast.219, f32[32,48]{1,0:T(8,128)S(1)} %broadcast_bitcast_fusion.2), kind=kLoop, calls=%fused_computation.17 | loop fusion | flops 2357760 | bytes 1191936 | tf_op jit(solution)/shard_map/reduce_sum | solution.py:124
  345.8 1.6 fusion.28
  348.4 0.7 fusion.72
  349.2 36.8 %all_gather.3 = bf16[64,3,2,512]{3,2,1,0:T(2,128)(2,1)S(1)} all-gather(bf16[4,3,2,512]{3,2,1,0:T(2,128)(2,1)S(1)} %get-tuple-element.79), channel_id=1, replica_groups=mesh['sec'=2,'seq'=32,'rep'=8] {'sec','rep'}, dimensions={0}, use_global_device_ids=true | all-gather | bytes 417792 | tf_op jit(solution)/shard_map/all_gather | solution.py:139
  386.7 3.1 collective-permute-start
  389.8 3.0 collective-permute-start.1
  392.8 3.5 collective-permute-done.1
  398.7 0.7 fusion.69
  400.1 0.7 fusion.67
  400.9 0.7 fusion.66
  402.3 0.7 fusion.40
  403.0 0.7 fusion.64
  404.4 0.7 fusion.48
  405.1 0.7 fusion.62
  406.6 0.7 fusion.45
  407.3 0.7 fusion.60
  408.0 0.7 fusion.59
  408.7 0.7 fusion.42
  409.4 0.7 fusion.58
  411.6 0.7 fusion.55
  413.7 0.7 fusion.52
  415.8 0.7 fusion.49
  416.5 7.9 %copy.123 = bf16[4,3,2,32,27,16]{3,2,1,0,5,4:T(2,128)(2,1)S(1)} copy(bf16[4,3,2,32,27,16]{5,3,2,1,0,4:T(8,128)(2,1)} %fusion.49) | data formatting | bytes 1327104 | tf_op jit(solution)/shard_map/stack | solution.py:80
  424.5 2.5 reshape_reshape.3
  427.0 1.7 convolution_add_fusion
  428.7 1.6 copy.124
  430.3 2.5 reshape.109
  432.8 2.7 reshape.110
  436.0 59.9 %psum.14 = f32[4,32]{1,0:T(4,128)S(1)} all-reduce(f32[4,32]{1,0:T(4,128)S(1)} %copy.125), channel_id=1, replica_groups=mesh['sec'=2,'seq'=32,'rep'=8] {'seq'}, use_global_device_ids=true, to_apply=%region_11.12 | all-reduce | flops 128 | bytes 1024 | tf_op jit(solution)/shard_map/psum | solution.py:151
  496.0 0.8 multiply_reduce_fusion.1
  496.8 62.3 %psum.15 = f32[4,32]{1,0:T(4,128)S(1)} all-reduce(f32[4,32]{1,0:T(4,128)S(1)} %copy.127), channel_id=1, replica_groups=mesh['sec'=2,'seq'=32,'rep'=8] {'seq'}, use_global_device_ids=true, to_apply=%region_13.14 | all-reduce | flops 128 | bytes 1024 | tf_op jit(solution)/shard_map/psum | solution.py:153
  559.5 2.5 mul.94
  562.3 2.5 sub.70
  564.8 4.5 fusion.20
  (104 shorter events, 24.5 us)
Async XLA Ops:
  0.6 426.3 %copy-start = (bf16[3,3,3,16,512]{4,3,2,1,0:T(8,128)(2,1)S(1)}, bf16[3,3,3,16,512]{4,3,2,1,0:T(8,128)(2,1)}, u32[]{:S(2)}) copy-start(bf16[3,3,3,16,512]{4,3,2,1,0:T(8,128)(2,1)} %param.28) | copy-start | bytes 1327108
  0.6 77.9 %copy-start.2 = (bf16[4,24,48,128]{3,2,1,0:T(8,128)(2,1)S(1)}, bf16[4,24,48,128]{3,2,1,0:T(8,128)(2,1)}, u32[]{:S(2)}) copy-start(bf16[4,24,48,128]{3,2,1,0:T(8,128)(2,1)} %param.19) | copy-start | bytes 3538948
  142.7 61.9 %all-to-all-start.2 = ((bf16[32,3,48,128]{3,2,1,0:T(8,128)(2,1)}), bf16[32,3,48,128]{3,2,1,0:T(8,128)(2,1)S(1)}, u32[]{:S(2)}, u32[]{:S(2)}) async-start(bf16[32,3,48,128]{3,2,1,0:T(8,128)(2,1)} %bitcast.14), calls=%async_computation.2 | async-start | bytes 2359296 | tf_op jit(solution)/shard_map/all_to_all | solution.py:116
  146.9 1.6 copy-start.1
  229.9 13.8 %copy-start.8 = (s32[64]{0:T(128)S(1)}, s32[64]{0:T(128)}, u32[]{:S(2)}) copy-start(s32[64]{0:T(128)} %param.27) | copy-start | bytes 772
  229.9 13.9 %copy-start.11 = (s32[4]{0:T(128)S(1)}, s32[4]{0:T(128)}, u32[]{:S(2)}) copy-start(s32[4]{0:T(128)} %param.26) | copy-start | bytes 52
  229.9 13.9 %copy-start.6 = (f32[512]{0:T(512)S(1)}, f32[512]{0:T(512)}, u32[]{:S(2)}) copy-start(f32[512]{0:T(512)} %param.31) | copy-start | bytes 6148
  229.9 14.0 %copy-start.3 = (f32[4,3072]{1,0:T(4,128)S(1)}, f32[4,3072]{1,0:T(4,128)}, u32[]{:S(2)}) copy-start(f32[4,3072]{1,0:T(4,128)} %param.22) | copy-start | bytes 147460
  229.9 14.0 %copy-start.4 = (f32[4,3072]{1,0:T(4,128)S(1)}, f32[4,3072]{1,0:T(4,128)}, u32[]{:S(2)}) copy-start(f32[4,3072]{1,0:T(4,128)} %param.21) | copy-start | bytes 147460
  238.1 82.0 %all-to-all-start.3 = ((bf16[1,3,1536,128]{3,1,0,2:T(4,128)(2,1)}), bf16[1,3,1536,128]{3,1,0,2:T(4,128)(2,1)S(1)}, u32[]{:S(2)}, u32[]{:S(2)}) async-start(bf16[1,3,1536,128]{3,1,0,2:T(4,128)(2,1)} %bitcast.224), calls=%async_computation.3 | async-start | bytes 3145728 | tf_op jit(solution)/shard_map/all_to_all | solution.py:118
  323.5 22.3 %copy-start.9 = (bf16[3072,64]{0,1:T(8,128)(2,1)S(1)}, bf16[3072,64]{0,1:T(8,128)(2,1)}, u32[]{:S(2)}) copy-start(bf16[3072,64]{0,1:T(8,128)(2,1)} %param.23) | copy-start | bytes 1179652
  323.5 22.3 %copy-start.12 = (f32[64]{0:T(128)S(1)}, f32[64]{0:T(128)}, u32[]{:S(2)}) copy-start(f32[64]{0:T(128)} %param.24) | copy-start | bytes 772
  323.7 24.7 %copy-start.5 = (f32[4,3,2,512]{3,2,1,0:T(2,128)S(1)}, f32[4,3,2,512]{3,2,1,0:T(2,128)}, u32[]{:S(2)}) copy-start(f32[4,3,2,512]{3,2,1,0:T(2,128)} %param.25) | copy-start | bytes 147460
  345.8 47.0 %copy-start.7 = (f32[512]{0:T(512)S(1)}, f32[512]{0:T(512)}, u32[]{:S(2)}) copy-start(f32[512]{0:T(512)} %param.30) | copy-start | bytes 6148
  386.7 6.2 %collective-permute-start = (bf16[4,3,1,512]{3,2,1,0:T(2,128)(2,1)S(1)}, bf16[4,3,1,512]{3,2,1,0:T(2,128)(2,1)S(1)}, u32[]{:S(2)}, u32[]{:S(2)}) collective-permute-start(bf16[4,3,1,512]{3,2,1,0:T(2,128)(2,1)S(1)} %get-tuple-element.89), channel_id=1, source_target_pairs={{0,8},{8,16},{16,24},{24,32},{32,40},{40,48},{48,56},{56,64},{64,7... | collective-permute-start | bytes 36872 | tf_op jit(solution)/shard_map/ppermute | solution.py:29
  389.8 6.6 %collective-permute-start.1 = (bf16[4,3,1,512]{3,2,1,0:T(2,128)(2,1)S(1)}, bf16[4,3,1,512]{3,2,1,0:T(2,128)(2,1)S(1)}, u32[]{:S(2)}, u32[]{:S(2)}) collective-permute-start(bf16[4,3,1,512]{3,2,1,0:T(2,128)(2,1)S(1)} %get-tuple-element.90), channel_id=1, source_target_pairs={{8,0},{16,8},{24,16},{32,24},{40,32},{48,40},{56,48},{64,56},{72,6... | collective-permute-start | bytes 36872 | tf_op jit(solution)/shard_map/ppermute | solution.py:31
  424.4 2.5 copy-start.10
where the time goes:
time: 570 us; the launch traced here: 569 us
  blocking collectives  301 us (53%)
  waiting for transfers between devices  135 us (24%)
  local copies, waits for them, and re-layouts  58.9 us (10%)
  other arithmetic  41.5 us (7%)
  matrix products  16.1 us (3%)
  starting transfers between devices  15.9 us (3%)
    all_to_all x1, blocking collectives, shards(): lax.all_to_all(query_four, 'seq', split_axis=0, concat_axis=2, tiled=True)  77.9 us
    all_to_all x1, waiting for transfers between devices, shards(): lax.all_to_all(outputs, 'seq', split_axis=2, concat_axis=0, tiled=True)  76.1 us
    all_to_all x1, blocking collectives, shards(): lax.all_to_all(keys_four, 'seq', split_axis=0, concat_axis=2, tiled=True)  64.2 us
    psum x1, blocking collectives, shards(): spread = lax.psum(jnp.sum(jnp.square(centered), axis=(1, 3)), 'seq') / cells  62.3 us
    psum x1, blocking collectives, shards(): mean = lax.psum(local_sum, 'seq') / cells  59.9 us
    all_to_all x1, waiting for transfers between devices, shards(): lax.all_to_all(values_four, 'seq', split_axis=0, concat_axis=2, tiled=True)  55 us
    all_gather x1, blocking collectives, shards(): everyone = lax.all_gather(decoder_in, ('sec', 'rep'), axis=0, tiled=True)  36.8 us
    reduce_sum x2, other arithmetic, shards(): spread = jnp.mean(jnp.square(heads - mean), axis=(1, 3), keepdims=True)  22 us
  transfers between devices with their start and end apart: 4, of which 3 were waited for; matrix products, arithmetic and copies ran while one was open for 0% of the time, Pallas kernels for 0%

commit v1 on v0

--- a/solution.py
+++ b/solution.py
@@ -1,3 +1,4 @@
+import functools
 import math
 import jax
 import jax.numpy as jnp
@@ -16,6 +17,15 @@
 LAT_W = 32
 eps_norm = 1e-06
 shift_factor = 7.0
+
+
+def _settle_things(t0, at_axis):
+    e_next = jnp.stack(lax.axis_size(("sec", "rep")) * [t0])
+    view_out = jnp.concatenate(lax.all_to_all(e_next, ("sec", "rep"), 0, 0), axis=at_axis)
+    return view_out
+
+
+_set_core = functools.partial(_settle_things, at_axis=0)
 
 
 def extended(cells, sides, width):
@@ -136,7 +146,7 @@
     decoder_in = denoised.astype(jnp.bfloat16)
     group_index = lax.axis_index(("sec", "rep"))
     wanted = lax.dynamic_slice_in_dim(clip_order, group_index * clips, clips)
-    everyone = lax.all_gather(decoder_in, ("sec", "rep"), axis=0, tiled=True)
+    everyone = _set_core(decoder_in)
     picked = jnp.take(everyone, wanted, axis=0)
     rimmed = edge_rows(extended(picked, (("seq", 2),), 1))
     columns = causal_columns(rimmed)

time: 570 us -> 552 us (0.968)
  blocking collectives: 301 us -> 264 us
  waiting for transfers between devices: 135 us -> 146 us
  starting transfers between devices: 15.9 us -> 22.3 us
    all_gather x1 -> x0, blocking collectives: 36.8 us -> none  [shards(): everyone = lax.all_gather(decoder_in, ('sec', 'rep'), axis=0, tiled=True)]
    all_to_all x0 -> x1, waiting for transfers between devices: none -> 10.8 us  [_settle_things(): lax.all_to_all(e_next, ('sec', 'rep'), 0, 0)]
    all_to_all x0 -> x1, starting transfers between devices: none -> 6.14 us  [_settle_things(): lax.all_to_all(e_next, ('sec', 'rep'), 0, 0)]
  transfers between devices with their start and end apart: 4 -> 5, of which waited for: 3 -> 4; matrix products, arithmetic and copies ran while one was open for 0% -> 0% of each run, Pallas kernels for 0% -> 0%
where the time goes in v1:
time: 552 us; the launch traced here: 551 us
  blocking collectives  264 us (48%)
  waiting for transfers between devices  146 us (26%)
  local copies, waits for them, and re-layouts  59.9 us (11%)
  other arithmetic  41.5 us (8%)
  starting transfers between devices  22.3 us (4%)
  matrix products  16.1 us (3%)
    all_to_all x1, blocking collectives, shards(): lax.all_to_all(query_four, 'seq', split_axis=0, concat_axis=2, tiled=True)  77.9 us
    all_to_all x1, waiting for transfers between devices, shards(): lax.all_to_all(outputs, 'seq', split_axis=2, concat_axis=0, tiled=True)  76.2 us
    all_to_all x1, blocking collectives, shards(): lax.all_to_all(keys_four, 'seq', split_axis=0, concat_axis=2, tiled=True)  64.2 us
    psum x1, blocking collectives, shards(): spread = lax.psum(jnp.sum(jnp.square(centered), axis=(1, 3)), 'seq') / cells  62.4 us
    psum x1, blocking collectives, shards(): mean = lax.psum(local_sum, 'seq') / cells  59.7 us
    all_to_all x1, waiting for transfers between devices, shards(): lax.all_to_all(values_four, 'seq', split_axis=0, concat_axis=2, tiled=True)  55 us
    reduce_sum x2, other arithmetic, shards(): spread = jnp.mean(jnp.square(heads - mean), axis=(1, 3), keepdims=True)  22 us
    unnamed x51, local copies, waits for them, and re-layouts  15.2 us
  transfers between devices with their start and end apart: 5, of which 4 were waited for; matrix products, arithmetic and copies ran while one was open for 0% of the time, Pallas kernels for 0%

profile of v1, /device:TPU:8, one launch (start us, length us, event | category | flops | bytes accessed | tf_op | source)
XLA Modules:
  0.0 551.1 jit_solution(3642542454033238650)
XLA Ops:
  0.7 77.9 %all_to_all.59 = bf16[32,3,48,128]{3,2,1,0:T(8,128)(2,1)} all-to-all(bf16[32,3,48,128]{3,2,1,0:T(8,128)(2,1)} %bitcast.228), channel_id=1, replica_groups=mesh['sec'=2,'seq'=32,'rep'=8] {'seq'}, dimensions={0} | all-to-all | bytes 2359296 | tf_op jit(solution)/shard_map/all_to_all | solution.py:124
  78.5 64.2 %all_to_all.60 = bf16[32,3,48,128]{3,2,1,0:T(8,128)(2,1)} all-to-all(bf16[32,3,48,128]{3,2,1,0:T(8,128)(2,1)S(1)} %bitcast.229), channel_id=1, replica_groups=mesh['sec'=2,'seq'=32,'rep'=8] {'seq'}, dimensions={0} | all-to-all | bytes 2359296 | tf_op jit(solution)/shard_map/all_to_all | solution.py:125
  142.7 4.2 all-to-all-start.2
  146.9 1.4 copy.116
  148.5 1.1 copy.117
  149.6 55.0 %all-to-all-done.2 = bf16[32,3,48,128]{3,2,1,0:T(8,128)(2,1)S(1)} async-done(((bf16[32,3,48,128]{3,2,1,0:T(8,128)(2,1)}), bf16[32,3,48,128]{3,2,1,0:T(8,128)(2,1)S(1)}, u32[]{:S(2)}, u32[]{:S(2)}) %all-to-all-start.2) | async-done | bytes 1179680 | tf_op jit(solution)/shard_map/all_to_all | solution.py:126
  204.6 1.1 copy.118
  205.8 24.2 %while.21 = (s32[]{:T(128)}, bf16[3,1536,128]{2,1,0:T(8,128)(2,1)}, bf16[3,1536,128]{2,1,0:T(8,128)(2,1)S(1)}, bf16[3,1536,128]{2,1,0:T(8,128)(2,1)}, bf16[3,153...) while((s32[]{:T(128)}, bf16[3,1536,128]{2,1,0:T(8,128)(2,1)}, ...), condition=%wide.region_5.6_spmd, body=%wide.region_0.5_spmd.sunk | while | flops 408222720 | bytes 13641974 | solution.py:127
  205.8 1.2 dynamic-slice_bitcast_fusion.3
  207.0 6.1 %while.22 = (s32[]{:T(128)}, bf16[3,512,128]{2,1,0:T(8,128)(2,1)S(1)}, bf16[3,512,128]{2,1,0:T(8,128)(2,1)S(1)}, bf16[1536,128]{1,0:T(8,128)(2,1)S(1)}, bf16[1536,128]{1,0:T(8,128)(2,1)S(1)}, /*index=5*/s32[]{:T(128)}) while((s32[]{:T(128)}, bf16[3,512,128]{2,1,0:T(8,128)(2,1)S(1)}, bf16[3,512,128]{2,1,0:T(8,128)(2,1)S(1)}, ...), condition=%wide.region_4.4_spmd, body=%wide.region_1.3_spmd.sunk | while | flops 408222720 | bytes 10496085 | solution.py:62
  208.2 0.8 fusion.89
  210.2 0.8 fusion.89
  212.2 0.8 fusion.89
  213.0 0.8 bitcast_dynamic-update-slice_fusion.2
  213.8 1.2 dynamic-slice_bitcast_fusion.3
  215.0 6.1 %while.22 = (s32[]{:T(128)}, bf16[3,512,128]{2,1,0:T(8,128)(2,1)S(1)}, bf16[3,512,128]{2,1,0:T(8,128)(2,1)S(1)}, bf16[1536,128]{1,0:T(8,128)(2,1)S(1)}, bf16[1536,128]{1,0:T(8,128)(2,1)S(1)}, /*index=5*/s32[]{:T(128)}) while((s32[]{:T(128)}, bf16[3,512,128]{2,1,0:T(8,128)(2,1)S(1)}, bf16[3,512,128]{2,1,0:T(8,128)(2,1)S(1)}, ...), condition=%wide.region_4.4_spmd, body=%wide.region_1.3_spmd.sunk | while | flops 408222720 | bytes 10496085 | solution.py:62
  216.2 0.8 fusion.89
  218.3 0.8 fusion.89
  220.3 0.8 fusion.89
  221.1 0.8 bitcast_dynamic-update-slice_fusion.2
  221.9 1.2 dynamic-slice_bitcast_fusion.3
  223.1 6.1 %while.22 = (s32[]{:T(128)}, bf16[3,512,128]{2,1,0:T(8,128)(2,1)S(1)}, bf16[3,512,128]{2,1,0:T(8,128)(2,1)S(1)}, bf16[1536,128]{1,0:T(8,128)(2,1)S(1)}, bf16[1536,128]{1,0:T(8,128)(2,1)S(1)}, /*index=5*/s32[]{:T(128)}) while((s32[]{:T(128)}, bf16[3,512,128]{2,1,0:T(8,128)(2,1)S(1)}, bf16[3,512,128]{2,1,0:T(8,128)(2,1)S(1)}, ...), condition=%wide.region_4.4_spmd, body=%wide.region_1.3_spmd.sunk | while | flops 408222720 | bytes 10496085 | solution.py:62
  224.3 0.8 fusion.89
  226.3 0.8 fusion.89
  228.4 0.8 fusion.89
  229.1 0.8 bitcast_dynamic-update-slice_fusion.2
  229.9 8.1 %copy.141 = bf16[3,1536,128]{2,0,1:T(4,128)(2,1)} copy(bf16[3,1536,128]{2,1,0:T(8,128)(2,1)} %get-tuple-element.56) | data formatting | bytes 2359296 | tf_op jit(solution)/shard_map/while | solution.py:127
  238.0 6.0 %all-to-all-start.3 = ((bf16[1,3,1536,128]{3,1,0,2:T(4,128)(2,1)}), bf16[1,3,1536,128]{3,1,0,2:T(4,128)(2,1)S(1)}, u32[]{:S(2)}, u32[]{:S(2)}) async-start(bf16[1,3,1536,128]{3,1,0,2:T(4,128)(2,1)} %bitcast.225), calls=%async_computation.3 | async-start | bytes 3145728 | tf_op jit(solution)/shard_map/all_to_all | solution.py:128
  244.1 76.2 %all-to-all-done.3 = bf16[1,3,1536,128]{3,1,0,2:T(4,128)(2,1)S(1)} async-done(((bf16[1,3,1536,128]{3,1,0,2:T(4,128)(2,1)}), bf16[1,3,1536,128]{3,1,0,2:T(4,128)(2,1)S(1)}, u32[]{:S(2)}, u32[]{:S(2)}) %all-to-all-start.3) | async-done | bytes 1179680 | tf_op jit(solution)/shard_map/all_to_all | solution.py:128
  320.6 3.1 fusion.19
  324.0 22.0 %multiply_reduce_fusion = f32[32,48]{1,0:T(8,128)S(1)} fusion(bf16[1,3,32,48,128]{4,1,3,2,0:T(4,128)(2,1)S(1)} %bitcast.220, f32[32,48]{1,0:T(8,128)S(1)} %broadcast_bitcast_fusion.2), kind=kLoop, calls=%fused_computation.17 | loop fusion | flops 2357760 | bytes 1191936 | tf_op jit(solution)/shard_map/reduce_sum | solution.py:134
  346.1 1.6 fusion.28
  348.7 0.7 fusion.72
  349.5 0.9 stack.103
  350.4 6.1 %all-to-all-start.4 = ((bf16[16,4,3,2,512]{4,3,2,1,0:T(2,128)(2,1)}), bf16[16,4,3,2,512]{4,3,2,1,0:T(2,128)(2,1)S(1)}, u32[]{:S(2)}, u32[]{:S(2)}) async-start(bf16[16,4,3,2,512]{4,3,2,1,0:T(2,128)(2,1)} %stack.103), calls=%async_computation.4 | async-start | bytes 786432 | tf_op jit(solution)/shard_map/all_to_all | solution.py:24
  356.7 10.8 %all-to-all-done.4 = bf16[16,4,3,2,512]{4,3,2,1,0:T(2,128)(2,1)S(1)} async-done(((bf16[16,4,3,2,512]{4,3,2,1,0:T(2,128)(2,1)}), bf16[16,4,3,2,512]{4,3,2,1,0:T(2,128)(2,1)S(1)}, u32[]{:S(2)}, u32[]{:S(2)}) %all-to-all-start.4) | async-done | bytes 393248 | tf_op jit(solution)/shard_map/all_to_all | solution.py:24
  368.3 3.2 collective-permute-start
  371.5 2.8 collective-permute-start.1
  374.4 3.7 collective-permute-done.1
  380.5 0.7 fusion.69
  381.9 0.7 fusion.67
  382.6 0.7 fusion.66
  384.0 0.7 fusion.40
  384.7 0.7 fusion.64
  386.2 0.7 fusion.48
  386.9 0.7 fusion.62
  389.0 0.7 fusion.60
  390.5 0.7 fusion.42
  391.2 0.7 fusion.58
  393.3 0.7 fusion.55
  395.4 0.7 fusion.52
  397.6 0.8 fusion.49
  398.3 7.9 %copy.123 = bf16[4,3,2,32,27,16]{3,2,1,0,5,4:T(2,128)(2,1)S(1)} copy(bf16[4,3,2,32,27,16]{5,3,2,1,0,4:T(8,128)(2,1)} %fusion.49) | data formatting | bytes 1327104 | tf_op jit(solution)/shard_map/stack | solution.py:90
  406.2 2.5 reshape_reshape.3
  408.7 1.7 convolution_add_fusion
  410.4 1.6 copy.124
  412.1 2.5 reshape.115
  414.5 2.7 reshape.116
  417.8 59.7 %psum.14 = f32[4,32]{1,0:T(4,128)S(1)} all-reduce(f32[4,32]{1,0:T(4,128)S(1)} %copy.125), channel_id=1, replica_groups=mesh['sec'=2,'seq'=32,'rep'=8] {'seq'}, use_global_device_ids=true, to_apply=%region_11.12 | all-reduce | flops 128 | bytes 1024 | tf_op jit(solution)/shard_map/psum | solution.py:161
  477.6 0.8 multiply_reduce_fusion.1
  478.4 62.4 %psum.15 = f32[4,32]{1,0:T(4,128)S(1)} all-reduce(f32[4,32]{1,0:T(4,128)S(1)} %copy.127), channel_id=1, replica_groups=mesh['sec'=2,'seq'=32,'rep'=8] {'seq'}, use_global_device_ids=true, to_apply=%region_13.14 | all-reduce | flops 128 | bytes 1024 | tf_op jit(solution)/shard_map/psum | solution.py:163
  541.2 2.5 mul.94
  544.1 2.5 sub.70
  546.6 4.5 fusion.20
  (106 shorter events, 25.9 us)
Async XLA Ops:
  0.6 408.1 %copy-start = (bf16[3,3,3,16,512]{4,3,2,1,0:T(8,128)(2,1)S(1)}, bf16[3,3,3,16,512]{4,3,2,1,0:T(8,128)(2,1)}, u32[]{:S(2)}) copy-start(bf16[3,3,3,16,512]{4,3,2,1,0:T(8,128)(2,1)} %param.28) | copy-start | bytes 1327108
  0.6 77.9 %copy-start.2 = (bf16[4,24,48,128]{3,2,1,0:T(8,128)(2,1)S(1)}, bf16[4,24,48,128]{3,2,1,0:T(8,128)(2,1)}, u32[]{:S(2)}) copy-start(bf16[4,24,48,128]{3,2,1,0:T(8,128)(2,1)} %param.19) | copy-start | bytes 3538948
  142.7 61.9 %all-to-all-start.2 = ((bf16[32,3,48,128]{3,2,1,0:T(8,128)(2,1)}), bf16[32,3,48,128]{3,2,1,0:T(8,128)(2,1)S(1)}, u32[]{:S(2)}, u32[]{:S(2)}) async-start(bf16[32,3,48,128]{3,2,1,0:T(8,128)(2,1)} %bitcast.14), calls=%async_computation.2 | async-start | bytes 2359296 | tf_op jit(solution)/shard_map/all_to_all | solution.py:126
  146.9 1.6 copy-start.1
  229.9 14.1 %copy-start.11 = (s32[4]{0:T(128)S(1)}, s32[4]{0:T(128)}, u32[]{:S(2)}) copy-start(s32[4]{0:T(128)} %param.26) | copy-start | bytes 52
  229.9 14.1 %copy-start.3 = (f32[4,3072]{1,0:T(4,128)S(1)}, f32[4,3072]{1,0:T(4,128)}, u32[]{:S(2)}) copy-start(f32[4,3072]{1,0:T(4,128)} %param.22) | copy-start | bytes 147460
  229.9 14.1 %copy-start.4 = (f32[4,3072]{1,0:T(4,128)S(1)}, f32[4,3072]{1,0:T(4,128)}, u32[]{:S(2)}) copy-start(f32[4,3072]{1,0:T(4,128)} %param.21) | copy-start | bytes 147460
  238.0 82.3 %all-to-all-start.3 = ((bf16[1,3,1536,128]{3,1,0,2:T(4,128)(2,1)}), bf16[1,3,1536,128]{3,1,0,2:T(4,128)(2,1)S(1)}, u32[]{:S(2)}, u32[]{:S(2)}) async-start(bf16[1,3,1536,128]{3,1,0,2:T(4,128)(2,1)} %bitcast.225), calls=%async_computation.3 | async-start | bytes 3145728 | tf_op jit(solution)/shard_map/all_to_all | solution.py:128
  323.7 22.3 %copy-start.9 = (bf16[3072,64]{0,1:T(8,128)(2,1)S(1)}, bf16[3072,64]{0,1:T(8,128)(2,1)}, u32[]{:S(2)}) copy-start(bf16[3072,64]{0,1:T(8,128)(2,1)} %param.23) | copy-start | bytes 1179652
  323.7 22.3 %copy-start.12 = (f32[64]{0:T(128)S(1)}, f32[64]{0:T(128)}, u32[]{:S(2)}) copy-start(f32[64]{0:T(128)} %param.24) | copy-start | bytes 772
  324.0 24.7 %copy-start.5 = (f32[4,3,2,512]{3,2,1,0:T(2,128)S(1)}, f32[4,3,2,512]{3,2,1,0:T(2,128)}, u32[]{:S(2)}) copy-start(f32[4,3,2,512]{3,2,1,0:T(2,128)} %param.25) | copy-start | bytes 147460
  346.1 10.5 %copy-start.8 = (s32[64]{0:T(128)S(1)}, s32[64]{0:T(128)}, u32[]{:S(2)}) copy-start(s32[64]{0:T(128)} %param.27) | copy-start | bytes 772
  346.1 10.6 %copy-start.6 = (f32[512]{0:T(512)S(1)}, f32[512]{0:T(512)}, u32[]{:S(2)}) copy-start(f32[512]{0:T(512)} %param.31) | copy-start | bytes 6148
  346.1 28.2 %copy-start.7 = (f32[512]{0:T(512)S(1)}, f32[512]{0:T(512)}, u32[]{:S(2)}) copy-start(f32[512]{0:T(512)} %param.30) | copy-start | bytes 6148
  350.4 17.1 %all-to-all-start.4 = ((bf16[16,4,3,2,512]{4,3,2,1,0:T(2,128)(2,1)}), bf16[16,4,3,2,512]{4,3,2,1,0:T(2,128)(2,1)S(1)}, u32[]{:S(2)}, u32[]{:S(2)}) async-start(bf16[16,4,3,2,512]{4,3,2,1,0:T(2,128)(2,1)} %stack.103), calls=%async_computation.4 | async-start | bytes 786432 | tf_op jit(solution)/shard_map/all_to_all | solution.py:24
  368.3 6.2 %collective-permute-start = (bf16[4,3,1,512]{3,2,1,0:T(2,128)(2,1)S(1)}, bf16[4,3,1,512]{3,2,1,0:T(2,128)(2,1)S(1)}, u32[]{:S(2)}, u32[]{:S(2)}) collective-permute-start(bf16[4,3,1,512]{3,2,1,0:T(2,128)(2,1)S(1)} %get-tuple-element.89), channel_id=1, source_target_pairs={{0,8},{8,16},{16,24},{24,32},{32,40},{40,48},{48,56},{56,64},{64,7... | collective-permute-start | bytes 36872 | tf_op jit(solution)/shard_map/ppermute | solution.py:39
  371.5 6.6 %collective-permute-start.1 = (bf16[4,3,1,512]{3,2,1,0:T(2,128)(2,1)S(1)}, bf16[4,3,1,512]{3,2,1,0:T(2,128)(2,1)S(1)}, u32[]{:S(2)}, u32[]{:S(2)}) collective-permute-start(bf16[4,3,1,512]{3,2,1,0:T(2,128)(2,1)S(1)} %get-tuple-element.90), channel_id=1, source_target_pairs={{8,0},{16,8},{24,16},{32,24},{40,32},{48,40},{56,48},{64,56},{72,6... | collective-permute-start | bytes 36872 | tf_op jit(solution)/shard_map/ppermute | solution.py:41
  406.2 2.5 copy-start.10
